TPU v7x, 256 devices: a whole 4x4x8 slice. The times are simulated.
256 devices in a mesh: tp: 8 (over x, core), ha: 8 (over y, z_lo), wa: 4 (over z_hi).
Axes of the slice: x: 4, y: 4, z: 8 (z_hi: 4, z_lo: 2; z = z_hi * 2 + z_lo), core: 2. Of those that a mesh axis runs over, the one named last changes fastest.
Arguments:
- queries: bfloat16 [1, 16, 8, 128, 3072], P(None, 'ha', 'wa', None, 'tp'), may hold values from -128 to 128
- keys: bfloat16 [1, 16, 8, 128, 3072], P(None, 'ha', 'wa', None, 'tp'), may hold values from -4.5 to 4.5
- values: bfloat16 [1, 16, 8, 128, 3072], P(None, 'ha', 'wa', None, 'tp'), may hold values from -6 to 6
- grad_out: bfloat16 [1, 16, 8, 128, 3072], P(None, 'ha', 'wa', None, 'tp'), may hold values from -6 to 6
- out_proj: bfloat16 [3072, 3072], P(('ha', 'wa'), 'tp'), may hold values from -0.109375 to 0.109375
Outputs:
- grad_queries: bfloat16 [1, 16, 8, 128, 3072], P(None, 'ha', 'wa', None, 'tp')
- grad_keys: bfloat16 [1, 16, 8, 128, 3072], P(None, 'ha', 'wa', None, 'tp')
- grad_values: bfloat16 [1, 16, 8, 128, 3072], P(None, 'ha', 'wa', None, 'tp')
All inputs are finite; a program needn't handle non-finite values.
Results may differ from a plain program's by a relative error of at most 0.014.
Values may be sent and summed in bfloat16 or wider, within the bound.
No kernel may reach another device: no remote copies, remote signals or barrier semaphores. Data moves between devices by JAX's collectives and lax.ppermute only.
A program may use at most 128 MiB of HBM per device.

v0:
```python
import jax
import jax.numpy as jnp
from jax import lax
from jax.sharding import PartitionSpec as P

HEAD = 128


def passed_along(value, axis, steps):
    count = lax.axis_size(axis)
    first, last = (max(0, -steps), min(count, count - steps))
    return lax.ppermute(value, axis, [(source, source + steps) for source in range(first, last)])


def extended_2(array, sides, width):
    for axis, dim in sides:
        peers, length = (lax.axis_size(axis), array.shape[dim])
        up = [(i, (i + 1) % peers) for i in range(peers - 1)]
        down = [(j, i) for i, j in up]
        last = lax.slice_in_dim(array, length - width, length, axis=dim)
        first = lax.slice_in_dim(array, 0, width, axis=dim)
        before = lax.ppermute(last, axis, up)
        after = lax.ppermute(first, axis, down)
        array = jnp.concatenate([before, array, after], axis=dim)
    return array


def tile_backward(query_blk, key_blk, value_blk, grad_blk, softmax_scale):
    f32 = jnp.float32
    scores = (
        jnp.einsum("qtd,qld->qtl", query_blk, key_blk, preferred_element_type=f32) * softmax_scale
    )
    scores = scores - jnp.max(scores, axis=-1, keepdims=True)
    expo = jnp.exp(scores)
    probs = expo / jnp.sum(expo, axis=-1, keepdims=True)
    probs_lo = probs.astype(jnp.bfloat16)
    attn = jnp.einsum("qtl,qld->qtd", probs_lo, value_blk, preferred_element_type=f32)
    delta = jnp.sum(grad_blk.astype(f32) * attn, axis=-1, keepdims=True)
    grad_probs = jnp.einsum("qtd,qld->qtl", grad_blk, value_blk, preferred_element_type=f32)
    grad_scores = (probs * (grad_probs - delta) * softmax_scale).astype(jnp.bfloat16)
    grad_query = jnp.einsum("qtl,qld->qtd", grad_scores, key_blk, preferred_element_type=f32)
    grad_key = jnp.einsum("qtl,qtd->qld", grad_scores, query_blk, preferred_element_type=f32)
    grad_value = jnp.einsum("qtl,qtd->qld", probs_lo, grad_blk, preferred_element_type=f32)
    return (grad_query, grad_key, grad_value)


def fold_cols(totals):
    from_left = passed_along(totals[:, :, :, -1].astype(jnp.bfloat16), "wa", 1).astype(jnp.float32)
    from_right = passed_along(totals[:, :, :, 0].astype(jnp.bfloat16), "wa", -1).astype(jnp.float32)
    inner = totals[:, :, :, 1:-1]
    inner = inner.at[:, :, :, 0].add(from_left)
    return inner.at[:, :, :, -1].add(from_right)


def fold_rows(totals):
    from_above = passed_along(totals[:, :, -1].astype(jnp.bfloat16), "ha", 1).astype(jnp.float32)
    from_below = passed_along(totals[:, :, 0].astype(jnp.bfloat16), "ha", -1).astype(jnp.float32)
    inner = totals[:, :, 1:-1]
    inner = inner.at[:, :, 0].add(from_above)
    return inner.at[:, :, -1].add(from_below)


def local(queries, keys, values, grad_out, out_proj):
    frames, tile_rows, tile_cols, tile_len, columns = queries.shape
    head_count = columns // HEAD
    whole = lax.all_gather(grad_out, "tp", axis=4, tiled=True)
    flat_rows = whole.reshape(-1, whole.shape[-1])
    grad_attn = jnp.dot(
        flat_rows,
        lax.all_gather(out_proj, ("ha", "wa"), axis=0, tiled=True),
        preferred_element_type=jnp.float32,
    )
    grad_attn = grad_attn.astype(jnp.bfloat16).reshape(queries.shape)
    stacked = jnp.stack([keys, values])
    extended = extended_2(stacked, (("ha", 2), ("wa", 3)), 1)
    row_base = lax.axis_index("ha") * tile_rows
    col_base = lax.axis_index("wa") * tile_cols
    rows_all = tile_rows * lax.axis_size("ha")
    cols_all = tile_cols * lax.axis_size("wa")
    span = min(3, frames)
    grid_f, grid_r, grid_c = jnp.meshgrid(
        jnp.arange(frames, dtype=jnp.int32),
        jnp.arange(tile_rows, dtype=jnp.int32),
        jnp.arange(tile_cols, dtype=jnp.int32),
        indexing="ij",
    )
    start_f = jnp.clip(grid_f.reshape(-1) - 1, 0, frames - span).astype(jnp.int32)
    start_r = (jnp.clip(row_base + grid_r.reshape(-1) - 1, 0, rows_all - 3) - row_base + 1).astype(
        jnp.int32
    )
    start_c = (jnp.clip(col_base + grid_c.reshape(-1) - 1, 0, cols_all - 3) - col_base + 1).astype(
        jnp.int32
    )
    tile_count = start_f.shape[0]
    zero_idx = jnp.zeros((), jnp.int32)
    softmax_scale = HEAD ** (-0.5)
    grad_q_parts = []
    total_parts = []
    for head_idx in range(head_count):
        lower = head_idx * HEAD
        both = extended[..., lower : lower + HEAD]

        def take(first, second, third):
            return lax.dynamic_slice(
                both,
                (zero_idx, first, second, third, zero_idx, zero_idx),
                (2, span, 3, 3, tile_len, HEAD),
            )

        window = jax.vmap(take)(start_f, start_r, start_c)
        key_blk = window[:, 0].reshape(tile_count, -1, HEAD)
        value_blk = window[:, 1].reshape(tile_count, -1, HEAD)
        query_blk = queries[..., lower : lower + HEAD].reshape(tile_count, tile_len, HEAD)
        grad_blk = grad_attn[..., lower : lower + HEAD].reshape(tile_count, tile_len, HEAD)
        grad_query, grad_key, grad_value = tile_backward(
            query_blk, key_blk, value_blk, grad_blk, softmax_scale
        )
        pieces = jnp.stack([grad_key, grad_value], 1).reshape(
            tile_count, 2, span, 3, 3, tile_len, HEAD
        )
        totals = jnp.zeros((2, frames, tile_rows + 2, tile_cols + 2, tile_len, HEAD), jnp.float32)

        def add_one(index, totals):
            start = (zero_idx, start_f[index], start_r[index], start_c[index], zero_idx, zero_idx)
            current = lax.dynamic_slice(totals, start, (2, span, 3, 3, tile_len, HEAD))
            return lax.dynamic_update_slice(totals, current + pieces[index], start)

        total_parts.append(lax.fori_loop(0, tile_count, add_one, totals))
        grad_q_parts.append(grad_query.reshape(frames, tile_rows, tile_cols, tile_len, HEAD))
    grad_queries = jnp.concatenate(grad_q_parts, axis=-1).astype(jnp.bfloat16)
    totals = jnp.concatenate(total_parts, axis=-1)
    folded = fold_rows(fold_cols(totals))
    return (grad_queries, folded[0].astype(jnp.bfloat16), folded[1].astype(jnp.bfloat16))


def solution(mesh):
    in_specs = (
        P(None, "ha", "wa", None, "tp"),
        P(None, "ha", "wa", None, "tp"),
        P(None, "ha", "wa", None, "tp"),
        P(None, "ha", "wa", None, "tp"),
        P(("ha", "wa"), "tp"),
    )
    out_specs = (
        P(None, "ha", "wa", None, "tp"),
        P(None, "ha", "wa", None, "tp"),
        P(None, "ha", "wa", None, "tp"),
    )
    return jax.shard_map(local, mesh=mesh, in_specs=in_specs, out_specs=out_specs, check_vma=False)
```

profile of v0, /device:TPU:64, one launch (start us, length us, event | category | flops | bytes accessed | tf_op | source)
XLA Modules:
  0.0 426.3 jit_solution(2551073699201183226)
XLA Ops:
  8.6 1.3 fusion.36
  10.0 1.3 collective-permute-start.1
  11.3 4.6 %collective-permute-start = (bf16[2,1,1,2,128,384]{5,4,0,1,3,2:T(8,128)(2,1)S(1)}, bf16[2,1,1,2,128,384]{5,4,0,1,3,2:T(8,128)(2,1)S(1)}, u32[]{:S(2)}, u32[]{:S(2)}) collective-permute-start(bf16[2,1,1,2,128,384]{5,4,0,1,3,2:T(8,128)(2,1)S(1)} %get-tuple-element.416), channel_id=1, source_target_pairs={{0,4},{4,8},{8,12},{12,16},{16,20},{20,24},{24,28},{1,5},{5,9},{9,... | collective-permute-start | bytes 1179656 | tf_op jit(solution)/shard_map/ppermute | solution.py:22
  15.8 8.0 %collective-permute-done.1 = bf16[2,1,1,2,128,384]{5,4,0,1,3,2:T(8,128)(2,1)S(1)} collective-permute-done((bf16[2,1,1,2,128,384]{5,4,0,1,3,2:T(8,128)(2,1)S(1)}, bf16[2,1,1,2,128,384]{5,4,0,1,3,2:T(8,128)(2,1)S(1)}, u32[]{:S(2)}, u32[]{:S(2)}) %collective-permute-start.1) | collective-permute-done | bytes 393248 | tf_op jit(solution)/shard_map/ppermute | solution.py:23
  23.8 1.9 collective-permute-done
  25.8 1.4 pad_maximum_fusion.5
  27.1 1.4 fusion.62
  28.5 1.9 collective-permute-start.3
  30.4 7.0 %collective-permute-start.2 = (bf16[2,1,4,1,128,384]{5,4,0,1,3,2:T(8,128)(2,1)}, bf16[2,1,4,1,128,384]{5,4,0,1,3,2:T(8,128)(2,1)S(1)}, u32[]{:S(2)}, u32[]{:S(2)}) collective-permute-start(bf16[2,1,4,1,128,384]{5,4,0,1,3,2:T(8,128)(2,1)} %get-tuple-element.412), channel_id=1, source_target_pairs={{0,1},{1,2},{2,3},{4,5},{5,6},{6,7},{8,9},{9,10},{10,11},{12,13},{... | collective-permute-start | bytes 2359304 | tf_op jit(solution)/shard_map/ppermute | solution.py:22
  37.9 1.8 fusion.63
  39.7 12.6 %collective-permute-done.3 = bf16[2,1,4,1,128,384]{5,4,0,1,3,2:T(8,128)(2,1)S(1)} collective-permute-done((bf16[2,1,4,1,128,384]{5,4,0,1,3,2:T(8,128)(2,1)}, bf16[2,1,4,1,128,384]{5,4,0,1,3,2:T(8,128)(2,1)S(1)}, u32[]{:S(2)}, u32[]{:S(2)}) %collective-permute-start.3) | collective-permute-done | bytes 786464 | tf_op jit(solution)/shard_map/ppermute | solution.py:23
  52.3 2.3 collective-permute-done.2
  56.1 2.3 gather_fusion.2
  58.4 2.3 gather_fusion.1
  61.7 3.6 fusion.61
  65.3 1.6 fusion.60
  66.8 1.6 fusion.59
  68.4 4.3 fusion.65
  72.7 2.3 fusion.66
  75.0 2.3 fusion.67
  77.3 106.3 %all-gather.5.cloned.1.call-done = bf16[3072,384]{1,0:T(8,128)(2,1)} async-done(((bf16[96,384]{1,0:T(8,128)(2,1)}), bf16[3072,384]{1,0:T(8,128)(2,1)}) %all-gather.5.cloned.1.call-update) | async-done | bytes 2359312 | tf_op jit(solution)/shard_map/all_gather | solution.py:70
  183.7 32.8 %all-gather.3.cloned.1.call-done = bf16[1,2,2,128,3072]{4,3,2,1,0:T(8,128)(2,1)} async-done(((bf16[1,2,2,128,384]{4,3,2,1,0:T(8,128)(2,1)}), bf16[1,2,2,128,3072]{4,3,2,1,0:T(8,128)(2,1)}) %all-gather.3.cloned.1.call-update) | async-done | bytes 3145744 | tf_op jit(solution)/shard_map/all_gather | solution.py:66
  216.4 4.4 %convolution_convert_fusion = bf16[512,384]{1,0:T(8,128)(2,1)S(1)} fusion(bf16[512,3072]{1,0:T(8,128)(2,1)} %bitcast.264, bf16[3072,384]{1,0:T(8,128)(2,1)} %all-gather.5.cloned.1.call-done), kind=kOutput, calls=%fused_computation.47 | convolution fusion | flops 1208156160 | bytes 5898240 | tf_op jit(solution)/shard_map/dot_general | solution.py:68
  221.6 4.0 fusion.49
  225.6 3.4 fusion.29
  229.0 3.6 fusion.52
  232.6 3.0 fusion.28
  235.7 3.6 fusion.55
  239.3 2.2 fusion.27
  241.5 2.6 fusion.21
  245.8 2.7 pad_maximum_fusion.3
  248.8 26.2 %while.45 = (s32[]{:T(128)}, f32[2,1,4,4,128,128]{5,4,3,2,1,0:T(8,128)S(1)}, s32[4]{0:T(128)S(1)}, s32[4]{0:T(128)S(1)}, f32[4,2,1,3,3,128,128]{6,5,4,3,1,2,0:T(8,128)}, /*index=5*/s32[]{:T(128)}, s32[]{:T(128)}, s32[]{:T(128)}) while((s32[]{:T(128)}, f32[2,1,4,4,128,128]{5,4,3,2,1,0:T(8,128)S(1)}, s32[4]{0:T(128)S(1)}, s32[4]{0:T(128)S(1)}, ...), condition=%wide.region_14.15_spmd, body=%wide.region_13.14_spmd.sunk | while | flops 294920 | bytes 3539141 | solution.py:128
  253.8 1.5 fusion.122
  260.4 1.5 fusion.122
  266.9 1.5 fusion.122
  273.5 1.5 fusion.122
  275.0 3.4 fusion.22
  280.5 2.7 pad_maximum_fusion.2
  283.5 26.2 %while.44 = (s32[]{:T(128)}, f32[2,1,4,4,128,128]{5,4,3,2,1,0:T(8,128)S(1)}, s32[4]{0:T(128)S(1)}, s32[4]{0:T(128)S(1)}, f32[4,2,1,3,3,128,128]{6,5,4,3,1,2,0:T(8,128)}, /*index=5*/s32[]{:T(128)}, s32[]{:T(128)}, s32[]{:T(128)}) while((s32[]{:T(128)}, f32[2,1,4,4,128,128]{5,4,3,2,1,0:T(8,128)S(1)}, s32[4]{0:T(128)S(1)}, s32[4]{0:T(128)S(1)}, ...), condition=%wide.region_12.13_spmd, body=%wide.region_11.12_spmd.sunk | while | flops 294920 | bytes 3539141 | solution.py:128
  288.5 1.5 fusion.121
  295.1 1.5 fusion.121
  301.7 1.5 fusion.121
  308.2 1.5 fusion.121
  309.7 3.3 fusion.23
  315.2 2.7 pad_maximum_fusion.1
  318.1 26.2 %while.43 = (s32[]{:T(128)}, f32[2,1,4,4,128,128]{5,4,3,2,1,0:T(8,128)S(1)}, s32[4]{0:T(128)S(1)}, s32[4]{0:T(128)S(1)}, f32[4,2,1,3,3,128,128]{6,5,4,3,1,2,0:T(8,128)}, /*index=5*/s32[]{:T(128)}, s32[]{:T(128)}, s32[]{:T(128)}) while((s32[]{:T(128)}, f32[2,1,4,4,128,128]{5,4,3,2,1,0:T(8,128)S(1)}, s32[4]{0:T(128)S(1)}, s32[4]{0:T(128)S(1)}, ...), condition=%wide.region_10.11_spmd, body=%wide.region_9.10_spmd.sunk | while | flops 294920 | bytes 3539141 | solution.py:128
  323.2 1.5 fusion.120
  329.7 1.5 fusion.120
  336.3 1.5 fusion.120
  342.8 1.5 fusion.120
  344.3 3.0 slice_bitcast_fusion.2
  347.3 5.6 %collective-permute-start.4 = (bf16[2,1,4,128,384]{4,3,0,2,1:T(8,128)(2,1)}, bf16[2,1,4,128,384]{4,3,0,2,1:T(8,128)(2,1)}, u32[]{:S(2)}, u32[]{:S(2)}) collective-permute-start(bf16[2,1,4,128,384]{4,3,0,2,1:T(8,128)(2,1)} %get-tuple-element.400), channel_id=1, source_target_pairs={{0,1},{1,2},{2,3},{4,5},{5,6},{6,7},{8,9},{9,10},{10,11},{12,13},{... | collective-permute-start | bytes 2359304 | tf_op jit(solution)/shard_map/ppermute | solution.py:12
  353.7 2.0 collective-permute-start.5
  355.7 2.2 convolution_convert_fusion.2
  358.0 2.6 pad_maximum_fusion
  361.2 26.1 %collective-permute-done.4 = bf16[2,1,4,128,384]{4,3,0,2,1:T(8,128)(2,1)} collective-permute-done((bf16[2,1,4,128,384]{4,3,0,2,1:T(8,128)(2,1)}, bf16[2,1,4,128,384]{4,3,0,2,1:T(8,128)(2,1)}, u32[]{:S(2)}, u32[]{:S(2)}) %collective-permute-start.4) | collective-permute-done | bytes 786464 | tf_op jit(solution)/shard_map/ppermute | solution.py:12
  387.3 1.3 fusion.26
  388.8 4.6 %collective-permute-done.5 = bf16[2,1,4,128,384]{4,3,0,2,1:T(8,128)(2,1)} collective-permute-done((bf16[2,1,4,128,384]{4,3,0,2,1:T(8,128)(2,1)}, bf16[2,1,4,128,384]{4,3,0,2,1:T(8,128)(2,1)}, u32[]{:S(2)}, u32[]{:S(2)}) %collective-permute-start.5) | collective-permute-done | bytes 786464 | tf_op jit(solution)/shard_map/ppermute | solution.py:12
  393.4 1.3 fusion.25
  395.9 4.1 collective-permute-start.6
  401.4 1.3 collective-permute-start.7
  402.7 1.7 pad_maximum_fusion.7
  404.5 1.8 collective-permute-done.6
  407.4 10.9 %collective-permute-done.7 = bf16[2,1,2,128,384]{4,3,2,0,1:T(8,128)(2,1)S(1)} collective-permute-done((bf16[2,1,2,128,384]{4,3,2,0,1:T(8,128)(2,1)}, bf16[2,1,2,128,384]{4,3,2,0,1:T(8,128)(2,1)S(1)}, u32[]{:S(2)}, u32[]{:S(2)}) %collective-permute-start.7) | collective-permute-done | bytes 393248 | tf_op jit(solution)/shard_map/ppermute | solution.py:12
  (118 shorter events, 32.3 us)
Async XLA Ops:
  7.2 176.5 %all-gather.5.cloned.1.call-start = ((), (), s32[]{:S(2)}) async-start(), calls=%async_computation.1 | async-start | bytes 2433024 | tf_op jit(solution)/shard_map/all_gather | solution.py:70
  7.9 208.5 %all-gather.3.cloned.1.call-start = ((), (), s32[]{:S(2)}) async-start(), calls=%async_computation | async-start | bytes 3538944 | tf_op jit(solution)/shard_map/all_gather | solution.py:66
  10.0 13.9 %collective-permute-start.1 = (bf16[2,1,1,2,128,384]{5,4,0,1,3,2:T(8,128)(2,1)S(1)}, bf16[2,1,1,2,128,384]{5,4,0,1,3,2:T(8,128)(2,1)S(1)}, u32[]{:S(2)}, u32[]{:S(2)}) collective-permute-start(bf16[2,1,1,2,128,384]{5,4,0,1,3,2:T(8,128)(2,1)S(1)} %get-tuple-element.417), channel_id=1, source_target_pairs={{4,0},{8,4},{12,8},{16,12},{20,16},{24,20},{28,24},{5,1},{9,5},{13... | collective-permute-start | bytes 1179656 | tf_op jit(solution)/shard_map/ppermute | solution.py:23
  11.3 14.5 %collective-permute-start = (bf16[2,1,1,2,128,384]{5,4,0,1,3,2:T(8,128)(2,1)S(1)}, bf16[2,1,1,2,128,384]{5,4,0,1,3,2:T(8,128)(2,1)S(1)}, u32[]{:S(2)}, u32[]{:S(2)}) collective-permute-start(bf16[2,1,1,2,128,384]{5,4,0,1,3,2:T(8,128)(2,1)S(1)} %get-tuple-element.416), channel_id=1, source_target_pairs={{0,4},{4,8},{8,12},{12,16},{16,20},{20,24},{24,28},{1,5},{5,9},{9,... | collective-permute-start | bytes 1179656 | tf_op jit(solution)/shard_map/ppermute | solution.py:22
  27.1 27.5 %copy-start.12 = (bf16[1,2,2,128,384]{4,3,2,1,0:T(8,128)(2,1)S(1)}, bf16[1,2,2,128,384]{4,3,2,1,0:T(8,128)(2,1)}, u32[]{:S(2)}) copy-start(bf16[1,2,2,128,384]{4,3,2,1,0:T(8,128)(2,1)} %param.20) | copy-start | bytes 1179652
  27.1 27.5 %copy-start.13 = (bf16[1,2,2,128,384]{4,3,2,1,0:T(8,128)(2,1)S(1)}, bf16[1,2,2,128,384]{4,3,2,1,0:T(8,128)(2,1)}, u32[]{:S(2)}) copy-start(bf16[1,2,2,128,384]{4,3,2,1,0:T(8,128)(2,1)} %param.21) | copy-start | bytes 1179652
  28.5 23.8 %collective-permute-start.3 = (bf16[2,1,4,1,128,384]{5,4,0,1,3,2:T(8,128)(2,1)}, bf16[2,1,4,1,128,384]{5,4,0,1,3,2:T(8,128)(2,1)S(1)}, u32[]{:S(2)}, u32[]{:S(2)}) collective-permute-start(bf16[2,1,4,1,128,384]{5,4,0,1,3,2:T(8,128)(2,1)} %get-tuple-element.413), channel_id=1, source_target_pairs={{1,0},{2,1},{3,2},{5,4},{6,5},{7,6},{9,8},{10,9},{11,10},{13,12},{... | collective-permute-start | bytes 2359304 | tf_op jit(solution)/shard_map/ppermute | solution.py:23
  30.4 24.2 %collective-permute-start.2 = (bf16[2,1,4,1,128,384]{5,4,0,1,3,2:T(8,128)(2,1)}, bf16[2,1,4,1,128,384]{5,4,0,1,3,2:T(8,128)(2,1)S(1)}, u32[]{:S(2)}, u32[]{:S(2)}) collective-permute-start(bf16[2,1,4,1,128,384]{5,4,0,1,3,2:T(8,128)(2,1)} %get-tuple-element.412), channel_id=1, source_target_pairs={{0,1},{1,2},{2,3},{4,5},{5,6},{6,7},{8,9},{9,10},{10,11},{12,13},{... | collective-permute-start | bytes 2359304 | tf_op jit(solution)/shard_map/ppermute | solution.py:22
  39.7 35.3 %copy-start.20 = (bf16[1,2,2,128,128]{4,3,2,1,0:T(8,128)(2,1)}, bf16[1,2,2,128,128]{4,3,2,1,0:T(8,128)(2,1)S(1)}, u32[]{:S(2)}) copy-start(bf16[1,2,2,128,128]{4,3,2,1,0:T(8,128)(2,1)S(1)} %get-tuple-element.418) | copy-start | bytes 393220
  61.7 3.6 copy-start.4
  66.8 1.6 copy-start.24
  68.4 4.3 %copy-start.10 = (bf16[4,1,1,3,3,128,128]{6,5,1,4,3,0,2:T(8,128)(2,1)S(1)}, bf16[4,1,1,3,3,128,128]{6,5,1,4,3,0,2:T(8,128)(2,1)}, u32[]{:S(2)}) copy-start(bf16[4,1,1,3,3,128,128]{6,5,1,4,3,0,2:T(8,128)(2,1)} %get-tuple-element.406) | copy-start | bytes 3538948
  68.4 4.3 %copy-start.22 = (bf16[1,2,2,128,128]{4,3,2,1,0:T(8,128)(2,1)S(1)}, bf16[1,2,2,128,128]{4,3,2,1,0:T(8,128)(2,1)}, u32[]{:S(2)}) copy-start(bf16[1,2,2,128,128]{4,3,2,1,0:T(8,128)(2,1)} %get-tuple-element.420) | copy-start | bytes 393220
  72.7 2.3 copy-start.8
  221.6 4.0 copy-start.19
  229.0 3.6 copy-start.18
  235.6 3.6 copy-start.17
  235.7 3.6 copy-start.21
  235.7 3.6 copy-start.26
  241.5 2.6 copy-start.25
  244.1 1.7 copy-start.16
  275.0 3.4 copy-start
  275.0 3.4 copy-start.23
  278.4 1.1 copy-start.5
  278.4 2.1 copy-start.15
  283.4 26.3 %copy-start.27 = (f32[4,128]{1,0:T(4,128)S(1)}, f32[4,128]{1,0:T(4,128)}, u32[]{:S(2)}) copy-start(f32[4,128]{1,0:T(4,128)} %fusion.27) | copy-start | bytes 6148
  309.7 3.4 copy-start.2
  313.1 1.0 copy-start.6
  313.1 2.1 copy-start.14
  344.3 8.7 %copy-start.11 = (bf16[4,1,1,3,3,128,128]{6,5,1,4,3,0,2:T(8,128)(2,1)S(1)}, bf16[4,1,1,3,3,128,128]{6,5,1,4,3,0,2:T(8,128)(2,1)}, u32[]{:S(2)}) copy-start(bf16[4,1,1,3,3,128,128]{6,5,1,4,3,0,2:T(8,128)(2,1)} %get-tuple-element.408) | copy-start | bytes 3538948
  347.3 39.9 %collective-permute-start.4 = (bf16[2,1,4,128,384]{4,3,0,2,1:T(8,128)(2,1)}, bf16[2,1,4,128,384]{4,3,0,2,1:T(8,128)(2,1)}, u32[]{:S(2)}, u32[]{:S(2)}) collective-permute-start(bf16[2,1,4,128,384]{4,3,0,2,1:T(8,128)(2,1)} %get-tuple-element.400), channel_id=1, source_target_pairs={{0,1},{1,2},{2,3},{4,5},{5,6},{6,7},{8,9},{9,10},{10,11},{12,13},{... | collective-permute-start | bytes 2359304 | tf_op jit(solution)/shard_map/ppermute | solution.py:12
  353.7 39.7 %collective-permute-start.5 = (bf16[2,1,4,128,384]{4,3,0,2,1:T(8,128)(2,1)}, bf16[2,1,4,128,384]{4,3,0,2,1:T(8,128)(2,1)}, u32[]{:S(2)}, u32[]{:S(2)}) collective-permute-start(bf16[2,1,4,128,384]{4,3,0,2,1:T(8,128)(2,1)} %get-tuple-element.399), channel_id=1, source_target_pairs={{1,0},{2,1},{3,2},{5,4},{6,5},{7,6},{9,8},{10,9},{11,10},{13,12},{... | collective-permute-start | bytes 2359304 | tf_op jit(solution)/shard_map/ppermute | solution.py:12
  360.9 26.4 %copy-start.1 = (f32[2,1,4,4,128,128]{5,4,3,2,1,0:T(8,128)S(1)}, f32[2,1,4,4,128,128]{5,4,3,2,1,0:T(8,128)}, u32[]{:S(2)}) copy-start(f32[2,1,4,4,128,128]{5,4,3,2,1,0:T(8,128)} %copy-done) | copy-start | bytes 6291460
  360.9 26.4 %copy-start.3 = (f32[2,1,4,4,128,128]{5,4,3,2,1,0:T(8,128)S(1)}, f32[2,1,4,4,128,128]{5,4,3,2,1,0:T(8,128)}, u32[]{:S(2)}) copy-start(f32[2,1,4,4,128,128]{5,4,3,2,1,0:T(8,128)} %copy-done.2) | copy-start | bytes 6291460
  394.7 5.3 %copy-start.7 = (bf16[4,128,1152]{1,2,0:T(8,128)(2,1)S(1)}, bf16[4,128,1152]{1,2,0:T(8,128)(2,1)}, u32[]{:S(2)}) copy-start(bf16[4,128,1152]{1,2,0:T(8,128)(2,1)} %copy-done.6) | copy-start | bytes 3538948
  394.7 5.3 %copy-start.9 = (bf16[4,1,1,3,3,128,128]{6,5,1,4,3,0,2:T(8,128)(2,1)S(1)}, bf16[4,1,1,3,3,128,128]{6,5,1,4,3,0,2:T(8,128)(2,1)}, u32[]{:S(2)}) copy-start(bf16[4,1,1,3,3,128,128]{6,5,1,4,3,0,2:T(8,128)(2,1)} %get-tuple-element.404) | copy-start | bytes 3538948
  395.9 10.3 %collective-permute-start.6 = (bf16[2,1,2,128,384]{4,3,2,0,1:T(8,128)(2,1)}, bf16[2,1,2,128,384]{4,3,2,0,1:T(8,128)(2,1)}, u32[]{:S(2)}, u32[]{:S(2)}) collective-permute-start(bf16[2,1,2,128,384]{4,3,2,0,1:T(8,128)(2,1)} %get-tuple-element.411), channel_id=1, source_target_pairs={{0,4},{4,8},{8,12},{12,16},{16,20},{20,24},{24,28},{1,5},{5,9},{9,... | collective-permute-start | bytes 1179656 | tf_op jit(solution)/shard_map/ppermute | solution.py:12
  401.4 17.0 %collective-permute-start.7 = (bf16[2,1,2,128,384]{4,3,2,0,1:T(8,128)(2,1)}, bf16[2,1,2,128,384]{4,3,2,0,1:T(8,128)(2,1)S(1)}, u32[]{:S(2)}, u32[]{:S(2)}) collective-permute-start(bf16[2,1,2,128,384]{4,3,2,0,1:T(8,128)(2,1)} %get-tuple-element.410), channel_id=1, source_target_pairs={{4,0},{8,4},{12,8},{16,12},{20,16},{24,20},{28,24},{5,1},{9,5},{13... | collective-permute-start | bytes 1179656 | tf_op jit(solution)/shard_map/ppermute | solution.py:12
Sparse Core Ops, SparseCore 0:
  9.8 173.8 all-gather.4
  185.5 30.8 all-gather.2
where the time goes:
time: 428 us; the launch traced here: 426 us
  waiting for transfers between devices  209 us (49%)
  matrix products  47.1 us (11%)
  loops' own time  46.9 us (11%)
  local copies, waits for them, and re-layouts  40.8 us (10%)
  other arithmetic  40.5 us (9%)
  starting transfers between devices  27.8 us (6%)
  between operations  14.5 us (3%)
    all_gather x1, waiting for transfers between devices, local(): lax.all_gather(out_proj, ('ha', 'wa'), axis=0, tiled=True)  106 us
    another operation x3, loops' own time, local(): total_parts.append(lax.fori_loop(0, tile_count, add_one, totals))  46.9 us
    ppermute x4, waiting for transfers between devices, passed_along(): lax.ppermute(value, axis, [(source, source + steps) for source in range(f...  43.4 us
    all_gather x1, waiting for transfers between devices, local(): whole = lax.all_gather(grad_out, 'tp', axis=4, tiled=True)  32.8 us
    ppermute x2, waiting for transfers between devices, extended_2(): after = lax.ppermute(first, axis, down)  20.6 us
    dynamic_update_slice x12, other arithmetic, add_one(): return lax.dynamic_update_slice(totals, current + pieces[index], start)  17.7 us
    ppermute x4, starting transfers between devices, passed_along(): lax.ppermute(value, axis, [(source, source + steps) for source in range(f...  13 us
    ppermute x2, starting transfers between devices, extended_2(): before = lax.ppermute(last, axis, up)  11.5 us
  transfers between devices with their start and end apart: 10, of which 10 were waited for; matrix products, arithmetic and copies ran while one was open for 10% of the time, Pallas kernels for 0%

commit v1 on v0

--- a/solution.py
+++ b/solution.py
@@ -61,9 +61,15 @@
 
 
 def local(queries, keys, values, grad_out, out_proj):
+
+    def _solve_panel(x_local, in_dim):
+        fresh = jnp.concatenate(jax.lax.axis_size("tp") * [x_local], axis=in_dim)
+        later = jax.lax.all_to_all(fresh, "tp", in_dim, in_dim, tiled=True)
+        return later
+
     frames, tile_rows, tile_cols, tile_len, columns = queries.shape
     head_count = columns // HEAD
-    whole = lax.all_gather(grad_out, "tp", axis=4, tiled=True)
+    whole = _solve_panel(grad_out, 4)
     flat_rows = whole.reshape(-1, whole.shape[-1])
     grad_attn = jnp.dot(
         flat_rows,

time: 428 us -> 377 us (0.88)
  waiting for transfers between devices: 209 us -> 116 us
  local copies, waits for them, and re-layouts: 40.8 us -> 62.9 us
  starting transfers between devices: 27.8 us -> 43.7 us
    all_gather x1 -> x0, waiting for transfers between devices: 32.8 us -> none  [local(): whole = lax.all_gather(grad_out, 'tp', axis=4, tiled=True)]
    ppermute x4, waiting for transfers between devices: 43.4 us -> 14.7 us  [passed_along(): lax.ppermute(value, axis, [(source, source + steps) for source in range(f...]
    all_gather x1, waiting for transfers between devices: 106 us -> 90.8 us  [local(): lax.all_gather(out_proj, ('ha', 'wa'), axis=0, tiled=True)]
    ppermute x2, waiting for transfers between devices: 20.6 us -> 7.39 us  [extended_2(): after = lax.ppermute(first, axis, down)]
    ppermute x4, starting transfers between devices: 13 us -> 23.5 us  [passed_along(): lax.ppermute(value, axis, [(source, source + steps) for source in range(f...]
    all_to_all x0 -> x1, local copies, waits for them, and re-layouts: none -> 6.87 us  [_solve_panel(): later = jax.lax.all_to_all(fresh, 'tp', in_dim, in_dim, tiled=True)]
    concatenate x0 -> x2, local copies, waits for them, and re-layouts: none -> 5.78 us  [_solve_panel(): fresh = jnp.concatenate(jax.lax.axis_size('tp') * [x_local], axis=in_dim)]
    gather x3, local copies, waits for them, and re-layouts: 5.58 us -> 10.4 us  [take(): lax.dynamic_slice(both, (zero_idx, first, second, third, zero_idx, zero_i...]
  transfers between devices with their start and end apart: 10 -> 10, of which waited for: 10 -> 9; matrix products, arithmetic and copies ran while one was open for 10% -> 18% of each run, Pallas kernels for 0% -> 0%
where the time goes in v1:
time: 377 us; the launch traced here: 375 us
  waiting for transfers between devices  116 us (31%)
  local copies, waits for them, and re-layouts  62.9 us (17%)
  matrix products  50.9 us (14%)
  loops' own time  45.3 us (12%)
  starting transfers between devices  43.7 us (12%)
  other arithmetic  41.6 us (11%)
  between operations  14.6 us (4%)
    all_gather x1, waiting for transfers between devices, local(): lax.all_gather(out_proj, ('ha', 'wa'), axis=0, tiled=True)  90.8 us
    another operation x3, loops' own time, local(): total_parts.append(lax.fori_loop(0, tile_count, add_one, totals))  45.3 us
    ppermute x4, starting transfers between devices, passed_along(): lax.ppermute(value, axis, [(source, source + steps) for source in range(f...  23.5 us
    dynamic_update_slice x12, other arithmetic, add_one(): return lax.dynamic_update_slice(totals, current + pieces[index], start)  17.7 us
    ppermute x4, waiting for transfers between devices, passed_along(): lax.ppermute(value, axis, [(source, source + steps) for source in range(f...  14.7 us
    dot_general x3, matrix products, tile_backward(): jnp.einsum('qtl,qtd->qld', probs_lo, grad_blk, preferred_element_type=f32)  11.8 us
    sub x3, matrix products, tile_backward(): scores = scores - jnp.max(scores, axis=-1, keepdims=True)  11.4 us
    ppermute x2, starting transfers between devices, extended_2(): before = lax.ppermute(last, axis, up)  11.3 us
  transfers between devices with their start and end apart: 10, of which 9 were waited for; matrix products, arithmetic and copies ran while one was open for 18% of the time, Pallas kernels for 0%

profile of v1, /device:TPU:64, one launch (start us, length us, event | category | flops | bytes accessed | tf_op | source)
XLA Modules:
  0.0 375.0 jit_solution(3443370388968799507)
XLA Ops:
  7.9 1.3 fusion.36
  9.2 1.3 collective-permute-start.1
  10.5 4.6 %collective-permute-start = (bf16[2,1,1,2,128,384]{5,4,0,1,3,2:T(8,128)(2,1)S(1)}, bf16[2,1,1,2,128,384]{5,4,0,1,3,2:T(8,128)(2,1)S(1)}, u32[]{:S(2)}, u32[]{:S(2)}) collective-permute-start(bf16[2,1,1,2,128,384]{5,4,0,1,3,2:T(8,128)(2,1)S(1)} %get-tuple-element.416), channel_id=1, source_target_pairs={{0,4},{4,8},{8,12},{12,16},{16,20},{20,24},{24,28},{1,5},{5,9},{9,... | collective-permute-start | bytes 1179656 | tf_op jit(solution)/shard_map/ppermute | solution.py:22
  16.8 6.3 %collective-permute-done.1 = bf16[2,1,1,2,128,384]{5,4,0,1,3,2:T(8,128)(2,1)S(1)} collective-permute-done((bf16[2,1,1,2,128,384]{5,4,0,1,3,2:T(8,128)(2,1)S(1)}, bf16[2,1,1,2,128,384]{5,4,0,1,3,2:T(8,128)(2,1)S(1)}, u32[]{:S(2)}, u32[]{:S(2)}) %collective-permute-start.1) | collective-permute-done | bytes 393248 | tf_op jit(solution)/shard_map/ppermute | solution.py:23
  23.7 1.3 fusion.62
  25.0 3.0 collective-permute-start.3
  28.0 6.8 %collective-permute-start.2 = (bf16[2,1,4,1,128,384]{5,4,0,1,3,2:T(8,128)(2,1)}, bf16[2,1,4,1,128,384]{5,4,0,1,3,2:T(8,128)(2,1)}, u32[]{:S(2)}, u32[]{:S(2)}) collective-permute-start(bf16[2,1,4,1,128,384]{5,4,0,1,3,2:T(8,128)(2,1)} %get-tuple-element.412), channel_id=1, source_target_pairs={{0,1},{1,2},{2,3},{4,5},{5,6},{6,7},{8,9},{9,10},{10,11},{12,13},{... | collective-permute-start | bytes 2359304 | tf_op jit(solution)/shard_map/ppermute | solution.py:22
  34.9 5.7 %copy.127 = bf16[1,2,2,128,3072]{3,2,1,0,4:T(2,128)(2,1)} copy(bf16[1,2,2,128,3072]{4,3,2,1,0:T(8,128)(2,1)S(1)} %constant_dynamic-update-slice_fusion) | data formatting | bytes 6291456 | tf_op jit(solution)/shard_map/concatenate | solution.py:66
  40.6 4.6 %all-to-all-start = ((bf16[1,2,2,128,3072]{3,2,1,0,4:T(2,128)(2,1)}), bf16[1,2,2,128,3072]{3,2,1,0,4:T(2,128)(2,1)S(1)}, u32[]{:S(2)}, u32[]{:S(2)}) async-start(bf16[1,2,2,128,3072]{3,2,1,0,4:T(2,128)(2,1)} %copy.127), calls=%async_computation | async-start | bytes 6291456 | tf_op jit(solution)/shard_map/all_to_all | solution.py:67
  47.1 1.8 fusion.63
  50.8 2.1 collective-permute-done.2
  52.8 2.0 pad_maximum_fusion.4
  54.9 2.1 fusion.58
  57.0 3.5 gather_fusion.2
  60.5 3.4 gather_fusion.1
  64.0 3.5 gather_fusion
  67.5 3.4 fusion.61
  70.9 1.6 fusion.60
  73.4 1.6 fusion.59
  75.0 4.2 %fusion.65 = (f32[4,128]{1,0:T(4,128)}, f32[4,128,1152]{1,2,0:T(8,128)}) fusion(bf16[4,1152,128]{2,1,0:T(8,128)(2,1)} %bitcast.220, bf16[4,128,128]{2,1,0:T(8,128)(2,1)S(1)} %bitcast.251), kind=kOutput, calls=%fused_computation.115 | convolution fusion | flops 152765568 | bytes 3672064 | tf_op jit(solution)/shard_map/sub | solution.py:33
  79.2 3.6 fusion.66
  82.8 3.6 fusion.67
  86.5 6.9 %copy.128 = bf16[1,2,2,128,3072]{4,3,2,1,0:T(8,128)(2,1)} copy(bf16[1,2,2,128,3072]{3,2,1,0,4:T(2,128)(2,1)S(1)} %all-to-all-done) | data formatting | bytes 6291456 | tf_op jit(solution)/shard_map/all_to_all | solution.py:67
  93.3 90.8 %all-gather.2.cloned.1.call-done = bf16[3072,384]{1,0:T(8,128)(2,1)} async-done(((bf16[96,384]{1,0:T(8,128)(2,1)}), bf16[3072,384]{1,0:T(8,128)(2,1)}) %all-gather.2.cloned.1.call-update) | async-done | bytes 2359312 | tf_op jit(solution)/shard_map/all_gather | solution.py:76
  184.2 4.4 %convolution_convert_fusion = bf16[512,384]{1,0:T(8,128)(2,1)S(1)} fusion(bf16[512,3072]{1,0:T(8,128)(2,1)} %bitcast.230, bf16[3072,384]{1,0:T(8,128)(2,1)} %all-gather.2.cloned.1.call-done), kind=kOutput, calls=%fused_computation.47 | convolution fusion | flops 1208156160 | bytes 5898240 | tf_op jit(solution)/shard_map/dot_general | solution.py:74
  188.7 3.9 %fusion.49 = f32[4,1152,128]{2,1,0:T(8,128)} fusion(bf16[4,128,128]{2,1,0:T(8,128)(2,1)S(1)} %bitcast.262, f32[4,128]{1,0:T(4,128)S(1)} %copy-done.30, bf16[4,1152,128]{2,1,0:T(8,128)(2,1)} %bitcast.221, bf16[4,128,128]{2,1,0:T(8,128)(2,1)S(1)} %bitcast.252), kind=kOutput, calls=%fused_computation.105 | convolution fusion | flops 304350848 | bytes 3803136 | tf_op jit(solution)/shard_map/qtl,qtd->qld/dot_general | solution.py:43
  192.6 2.8 fusion.29
  195.4 3.9 %fusion.52 = f32[4,1152,128]{2,1,0:T(8,128)} fusion(bf16[4,128,128]{2,1,0:T(8,128)(2,1)S(1)} %bitcast.259, f32[4,128]{1,0:T(4,128)S(1)} %get-tuple-element.426, bf16[4,1152,128]{2,1,0:T(8,128)(2,1)} %bitcast.217, bf16[4,128,128]{2,1,0:T(8,128)(2,1)S(1)} %bitcast.248), kind=kOutput, calls=%fused_computation.106 | convolution fusion | flops 304350848 | bytes 3803136 | tf_op jit(solution)/shard_map/qtl,qtd->qld/dot_general | solution.py:43
  199.3 3.3 fusion.28
  202.6 4.0 %fusion.55 = f32[4,1152,128]{2,1,0:T(8,128)} fusion(bf16[4,128,128]{2,1,0:T(8,128)(2,1)S(1)} %bitcast.256, f32[4,128]{1,0:T(4,128)S(1)} %get-tuple-element.428, bf16[4,1152,128]{2,1,0:T(8,128)(2,1)} %bitcast.213, bf16[4,128,128]{2,1,0:T(8,128)(2,1)S(1)} %bitcast.244), kind=kOutput, calls=%fused_computation.107 | convolution fusion | flops 304350848 | bytes 3803136 | tf_op jit(solution)/shard_map/qtl,qtd->qld/dot_general | solution.py:43
  206.6 3.3 fusion.27
  209.9 2.6 fusion.21
  214.2 2.7 pad_maximum_fusion.3
  217.2 24.4 %while.45 = (s32[]{:T(128)}, f32[2,1,4,4,128,128]{5,4,3,2,1,0:T(8,128)S(1)}, s32[4]{0:T(128)S(1)}, s32[4]{0:T(128)S(1)}, f32[4,2,1,3,3,128,128]{6,5,4,3,1,2,0:T(8,128)}, /*index=5*/s32[]{:T(128)}, s32[]{:T(128)}, s32[]{:T(128)}) while((s32[]{:T(128)}, f32[2,1,4,4,128,128]{5,4,3,2,1,0:T(8,128)S(1)}, s32[4]{0:T(128)S(1)}, s32[4]{0:T(128)S(1)}, ...), condition=%wide.region_14.15_spmd, body=%wide.region_13.14_spmd.sunk | while | flops 294920 | bytes 3539141 | solution.py:134
  221.8 1.5 fusion.122
  227.9 1.5 fusion.122
  234.0 1.5 fusion.122
  240.1 1.5 fusion.122
  241.6 3.4 fusion.22
  247.1 2.7 pad_maximum_fusion.2
  250.1 26.4 %while.44 = (s32[]{:T(128)}, f32[2,1,4,4,128,128]{5,4,3,2,1,0:T(8,128)S(1)}, s32[4]{0:T(128)S(1)}, s32[4]{0:T(128)S(1)}, f32[4,2,1,3,3,128,128]{6,5,4,3,1,2,0:T(8,128)}, /*index=5*/s32[]{:T(128)}, s32[]{:T(128)}, s32[]{:T(128)}) while((s32[]{:T(128)}, f32[2,1,4,4,128,128]{5,4,3,2,1,0:T(8,128)S(1)}, s32[4]{0:T(128)S(1)}, s32[4]{0:T(128)S(1)}, ...), condition=%wide.region_12.13_spmd, body=%wide.region_11.12_spmd.sunk | while | flops 294920 | bytes 3539141 | solution.py:134
  255.1 1.5 fusion.121
  261.7 1.5 fusion.121
  268.2 1.5 fusion.121
  274.8 1.5 fusion.121
  276.5 3.3 fusion.23
  282.0 2.8 pad_maximum_fusion.1
  285.0 26.2 %while.43 = (s32[]{:T(128)}, f32[2,1,4,4,128,128]{5,4,3,2,1,0:T(8,128)S(1)}, s32[4]{0:T(128)S(1)}, s32[4]{0:T(128)S(1)}, f32[4,2,1,3,3,128,128]{6,5,4,3,1,2,0:T(8,128)}, /*index=5*/s32[]{:T(128)}, s32[]{:T(128)}, s32[]{:T(128)}) while((s32[]{:T(128)}, f32[2,1,4,4,128,128]{5,4,3,2,1,0:T(8,128)S(1)}, s32[4]{0:T(128)S(1)}, s32[4]{0:T(128)S(1)}, ...), condition=%wide.region_10.11_spmd, body=%wide.region_9.10_spmd.sunk | while | flops 294920 | bytes 3539141 | solution.py:134
  290.0 1.5 fusion.120
  296.6 1.5 fusion.120
  303.2 1.5 fusion.120
  309.7 1.5 fusion.120
  311.2 3.0 slice_bitcast_fusion.2
  314.2 3.4 collective-permute-start.4
  318.3 4.2 %collective-permute-start.5 = (bf16[2,1,4,128,384]{4,3,0,2,1:T(8,128)(2,1)}, bf16[2,1,4,128,384]{4,3,0,2,1:T(8,128)(2,1)}, u32[]{:S(2)}, u32[]{:S(2)}) collective-permute-start(bf16[2,1,4,128,384]{4,3,0,2,1:T(8,128)(2,1)} %get-tuple-element.399), channel_id=1, source_target_pairs={{1,0},{2,1},{3,2},{5,4},{6,5},{7,6},{9,8},{10,9},{11,10},{13,12},{... | collective-permute-start | bytes 2359304 | tf_op jit(solution)/shard_map/ppermute | solution.py:12
  322.6 2.2 convolution_convert_fusion.2
  324.9 2.6 pad_maximum_fusion
  328.1 8.1 %collective-permute-done.4 = bf16[2,1,4,128,384]{4,3,0,2,1:T(8,128)(2,1)} collective-permute-done((bf16[2,1,4,128,384]{4,3,0,2,1:T(8,128)(2,1)}, bf16[2,1,4,128,384]{4,3,0,2,1:T(8,128)(2,1)}, u32[]{:S(2)}, u32[]{:S(2)}) %collective-permute-start.4) | collective-permute-done | bytes 786464 | tf_op jit(solution)/shard_map/ppermute | solution.py:12
  336.2 1.3 fusion.26
  338.7 1.3 fusion.25
  341.2 14.6 %collective-permute-start.6 = (bf16[2,1,2,128,384]{4,3,2,0,1:T(8,128)(2,1)}, bf16[2,1,2,128,384]{4,3,2,0,1:T(8,128)(2,1)}, u32[]{:S(2)}, u32[]{:S(2)}) collective-permute-start(bf16[2,1,2,128,384]{4,3,2,0,1:T(8,128)(2,1)} %get-tuple-element.411), channel_id=1, source_target_pairs={{0,4},{4,8},{8,12},{12,16},{16,20},{20,24},{24,28},{1,5},{5,9},{9,... | collective-permute-start | bytes 1179656 | tf_op jit(solution)/shard_map/ppermute | solution.py:12
  357.2 1.3 collective-permute-start.7
  358.5 1.7 pad_maximum_fusion.7
  361.9 5.2 %collective-permute-done.7 = bf16[2,1,2,128,384]{4,3,2,0,1:T(8,128)(2,1)S(1)} collective-permute-done((bf16[2,1,2,128,384]{4,3,2,0,1:T(8,128)(2,1)}, bf16[2,1,2,128,384]{4,3,2,0,1:T(8,128)(2,1)S(1)}, u32[]{:S(2)}, u32[]{:S(2)}) %collective-permute-start.7) | collective-permute-done | bytes 393248 | tf_op jit(solution)/shard_map/ppermute | solution.py:12
  (135 shorter events, 36.4 us)
Async XLA Ops:
  7.2 9.0 %copy-start.4 = (bf16[1,2,2,128,384]{4,3,2,1,0:T(8,128)(2,1)S(1)}, bf16[1,2,2,128,384]{4,3,2,1,0:T(8,128)(2,1)}, u32[]{:S(2)}) copy-start(bf16[1,2,2,128,384]{4,3,2,1,0:T(8,128)(2,1)} %param.22) | copy-start | bytes 1179652
  7.2 177.0 %all-gather.2.cloned.1.call-start = ((), (), s32[]{:S(2)}) async-start(), calls=%async_computation.1 | async-start | bytes 2433024 | tf_op jit(solution)/shard_map/all_gather | solution.py:76
  9.2 13.9 %collective-permute-start.1 = (bf16[2,1,1,2,128,384]{5,4,0,1,3,2:T(8,128)(2,1)S(1)}, bf16[2,1,1,2,128,384]{5,4,0,1,3,2:T(8,128)(2,1)S(1)}, u32[]{:S(2)}, u32[]{:S(2)}) collective-permute-start(bf16[2,1,1,2,128,384]{5,4,0,1,3,2:T(8,128)(2,1)S(1)} %get-tuple-element.417), channel_id=1, source_target_pairs={{4,0},{8,4},{12,8},{16,12},{20,16},{24,20},{28,24},{5,1},{9,5},{13... | collective-permute-start | bytes 1179656 | tf_op jit(solution)/shard_map/ppermute | solution.py:23
  10.5 12.9 %collective-permute-start = (bf16[2,1,1,2,128,384]{5,4,0,1,3,2:T(8,128)(2,1)S(1)}, bf16[2,1,1,2,128,384]{5,4,0,1,3,2:T(8,128)(2,1)S(1)}, u32[]{:S(2)}, u32[]{:S(2)}) collective-permute-start(bf16[2,1,1,2,128,384]{5,4,0,1,3,2:T(8,128)(2,1)S(1)} %get-tuple-element.416), channel_id=1, source_target_pairs={{0,4},{4,8},{8,12},{12,16},{16,20},{20,24},{24,28},{1,5},{5,9},{9,... | collective-permute-start | bytes 1179656 | tf_op jit(solution)/shard_map/ppermute | solution.py:22
  16.2 7.3 %copy-start.12 = (bf16[1,2,2,128,384]{4,3,2,1,0:T(8,128)(2,1)S(1)}, bf16[1,2,2,128,384]{4,3,2,1,0:T(8,128)(2,1)}, u32[]{:S(2)}) copy-start(bf16[1,2,2,128,384]{4,3,2,1,0:T(8,128)(2,1)} %param.20) | copy-start | bytes 1179652
  16.2 7.2 %copy-start.14 = (bf16[1,2,2,128,384]{4,3,2,1,0:T(8,128)(2,1)S(1)}, bf16[1,2,2,128,384]{4,3,2,1,0:T(8,128)(2,1)}, u32[]{:S(2)}) copy-start(bf16[1,2,2,128,384]{4,3,2,1,0:T(8,128)(2,1)} %param.21) | copy-start | bytes 1179652
  23.1 1.9 copy-start.18
  23.4 1.6 copy-start.19
  25.0 25.7 %collective-permute-start.3 = (bf16[2,1,4,1,128,384]{5,4,0,1,3,2:T(8,128)(2,1)}, bf16[2,1,4,1,128,384]{5,4,0,1,3,2:T(8,128)(2,1)}, u32[]{:S(2)}, u32[]{:S(2)}) collective-permute-start(bf16[2,1,4,1,128,384]{5,4,0,1,3,2:T(8,128)(2,1)} %get-tuple-element.413), channel_id=1, source_target_pairs={{1,0},{2,1},{3,2},{5,4},{6,5},{7,6},{9,8},{10,9},{11,10},{13,12},{... | collective-permute-start | bytes 2359304 | tf_op jit(solution)/shard_map/ppermute | solution.py:23
  28.0 24.8 %collective-permute-start.2 = (bf16[2,1,4,1,128,384]{5,4,0,1,3,2:T(8,128)(2,1)}, bf16[2,1,4,1,128,384]{5,4,0,1,3,2:T(8,128)(2,1)}, u32[]{:S(2)}, u32[]{:S(2)}) collective-permute-start(bf16[2,1,4,1,128,384]{5,4,0,1,3,2:T(8,128)(2,1)} %get-tuple-element.412), channel_id=1, source_target_pairs={{0,1},{1,2},{2,3},{4,5},{5,6},{6,7},{8,9},{9,10},{10,11},{12,13},{... | collective-permute-start | bytes 2359304 | tf_op jit(solution)/shard_map/ppermute | solution.py:22
  40.6 12.3 %copy-start.13 = (bf16[1,2,2,128,384]{4,3,2,1,0:T(8,128)(2,1)S(1)}, bf16[1,2,2,128,384]{4,3,2,1,0:T(8,128)(2,1)}, u32[]{:S(2)}) copy-start(bf16[1,2,2,128,384]{4,3,2,1,0:T(8,128)(2,1)} %param.20) | copy-start | bytes 1179652
  40.6 45.9 %all-to-all-start = ((bf16[1,2,2,128,3072]{3,2,1,0,4:T(2,128)(2,1)}), bf16[1,2,2,128,3072]{3,2,1,0,4:T(2,128)(2,1)S(1)}, u32[]{:S(2)}, u32[]{:S(2)}) async-start(bf16[1,2,2,128,3072]{3,2,1,0,4:T(2,128)(2,1)} %copy.127), calls=%async_computation | async-start | bytes 6291456 | tf_op jit(solution)/shard_map/all_to_all | solution.py:67
  67.5 3.4 copy-start.6
  70.9 2.5 copy-start.5
  73.4 1.6 copy-start.25
  75.0 4.2 %copy-start.24 = (bf16[1,2,2,128,128]{4,3,2,1,0:T(8,128)(2,1)S(1)}, bf16[1,2,2,128,128]{4,3,2,1,0:T(8,128)(2,1)}, u32[]{:S(2)}) copy-start(bf16[1,2,2,128,128]{4,3,2,1,0:T(8,128)(2,1)} %get-tuple-element.420) | copy-start | bytes 393220
  79.2 3.6 copy-start.23
  184.2 4.5 %copy-start.30 = (f32[4,128]{1,0:T(4,128)S(1)}, f32[4,128]{1,0:T(4,128)}, u32[]{:S(2)}) copy-start(f32[4,128]{1,0:T(4,128)} %get-tuple-element.424) | copy-start | bytes 6148
  188.7 10.6 %copy-start.29 = (bf16[1,2,2,128,128]{4,3,2,1,0:T(8,128)(2,1)}, bf16[1,2,2,128,128]{4,3,2,1,0:T(8,128)(2,1)S(1)}, u32[]{:S(2)}) copy-start(bf16[1,2,2,128,128]{4,3,2,1,0:T(8,128)(2,1)S(1)} %get-tuple-element.423) | copy-start | bytes 393220
  188.7 17.9 %copy-start.27 = (bf16[1,2,2,128,128]{4,3,2,1,0:T(8,128)(2,1)}, bf16[1,2,2,128,128]{4,3,2,1,0:T(8,128)(2,1)S(1)}, u32[]{:S(2)}) copy-start(bf16[1,2,2,128,128]{4,3,2,1,0:T(8,128)(2,1)S(1)} %get-tuple-element.421) | copy-start | bytes 393220
  188.7 3.9 %copy-start.22 = (bf16[4,1,1,3,3,128,128]{6,5,1,4,3,0,2:T(8,128)(2,1)S(1)}, bf16[4,1,1,3,3,128,128]{6,5,1,4,3,0,2:T(8,128)(2,1)}, u32[]{:S(2)}) copy-start(bf16[4,1,1,3,3,128,128]{6,5,1,4,3,0,2:T(8,128)(2,1)} %get-tuple-element.409) | copy-start | bytes 3538948
  195.4 3.9 %copy-start.21 = (bf16[4,1,1,3,3,128,128]{6,5,1,4,3,0,2:T(8,128)(2,1)S(1)}, bf16[4,1,1,3,3,128,128]{6,5,1,4,3,0,2:T(8,128)(2,1)}, u32[]{:S(2)}) copy-start(bf16[4,1,1,3,3,128,128]{6,5,1,4,3,0,2:T(8,128)(2,1)} %get-tuple-element.407) | copy-start | bytes 3538948
  202.6 4.0 %copy-start.20 = (bf16[4,1,1,3,3,128,128]{6,5,1,4,3,0,2:T(8,128)(2,1)S(1)}, bf16[4,1,1,3,3,128,128]{6,5,1,4,3,0,2:T(8,128)(2,1)}, u32[]{:S(2)}) copy-start(bf16[4,1,1,3,3,128,128]{6,5,1,4,3,0,2:T(8,128)(2,1)} %get-tuple-element.405) | copy-start | bytes 3538948
  209.9 2.6 copy-start.26
  212.5 1.7 copy-start.17
  241.6 3.4 copy-start
  245.0 1.1 copy-start.7
  245.0 2.1 copy-start.16
  250.0 26.5 %copy-start.28 = (bf16[1,2,2,128,128]{4,3,2,1,0:T(8,128)(2,1)S(1)}, bf16[1,2,2,128,128]{4,3,2,1,0:T(8,128)(2,1)}, u32[]{:S(2)}) copy-start(bf16[1,2,2,128,128]{4,3,2,1,0:T(8,128)(2,1)} %copy-done.27) | copy-start | bytes 393220
  250.0 26.5 %copy-start.31 = (f32[4,128]{1,0:T(4,128)S(1)}, f32[4,128]{1,0:T(4,128)}, u32[]{:S(2)}) copy-start(f32[4,128]{1,0:T(4,128)} %fusion.27) | copy-start | bytes 6148
  276.5 3.4 copy-start.2
  279.9 1.0 copy-start.8
  279.9 2.1 copy-start.15
  311.2 6.4 %copy-start.11 = (bf16[4,1,1,3,3,128,128]{6,5,1,4,3,0,2:T(8,128)(2,1)S(1)}, bf16[4,1,1,3,3,128,128]{6,5,1,4,3,0,2:T(8,128)(2,1)}, u32[]{:S(2)}) copy-start(bf16[4,1,1,3,3,128,128]{6,5,1,4,3,0,2:T(8,128)(2,1)} %get-tuple-element.408) | copy-start | bytes 3538948
  314.2 21.9 %collective-permute-start.4 = (bf16[2,1,4,128,384]{4,3,0,2,1:T(8,128)(2,1)}, bf16[2,1,4,128,384]{4,3,0,2,1:T(8,128)(2,1)}, u32[]{:S(2)}, u32[]{:S(2)}) collective-permute-start(bf16[2,1,4,128,384]{4,3,0,2,1:T(8,128)(2,1)} %get-tuple-element.400), channel_id=1, source_target_pairs={{0,1},{1,2},{2,3},{4,5},{5,6},{6,7},{8,9},{9,10},{10,11},{12,13},{... | collective-permute-start | bytes 2359304 | tf_op jit(solution)/shard_map/ppermute | solution.py:12
  318.3 20.4 %collective-permute-start.5 = (bf16[2,1,4,128,384]{4,3,0,2,1:T(8,128)(2,1)}, bf16[2,1,4,128,384]{4,3,0,2,1:T(8,128)(2,1)}, u32[]{:S(2)}, u32[]{:S(2)}) collective-permute-start(bf16[2,1,4,128,384]{4,3,0,2,1:T(8,128)(2,1)} %get-tuple-element.399), channel_id=1, source_target_pairs={{1,0},{2,1},{3,2},{5,4},{6,5},{7,6},{9,8},{10,9},{11,10},{13,12},{... | collective-permute-start | bytes 2359304 | tf_op jit(solution)/shard_map/ppermute | solution.py:12
  327.8 8.4 %copy-start.1 = (f32[2,1,4,4,128,128]{5,4,3,2,1,0:T(8,128)S(1)}, f32[2,1,4,4,128,128]{5,4,3,2,1,0:T(8,128)}, u32[]{:S(2)}) copy-start(f32[2,1,4,4,128,128]{5,4,3,2,1,0:T(8,128)} %copy-done) | copy-start | bytes 6291460
  327.8 8.4 %copy-start.3 = (f32[2,1,4,4,128,128]{5,4,3,2,1,0:T(8,128)S(1)}, f32[2,1,4,4,128,128]{5,4,3,2,1,0:T(8,128)}, u32[]{:S(2)}) copy-start(f32[2,1,4,4,128,128]{5,4,3,2,1,0:T(8,128)} %copy-done.2) | copy-start | bytes 6291460
  340.0 15.9 %copy-start.9 = (bf16[4,128,1152]{1,2,0:T(8,128)(2,1)S(1)}, bf16[4,128,1152]{1,2,0:T(8,128)(2,1)}, u32[]{:S(2)}) copy-start(bf16[4,128,1152]{1,2,0:T(8,128)(2,1)} %copy-done.8) | copy-start | bytes 3538948
  340.0 15.9 %copy-start.10 = (bf16[4,1,1,3,3,128,128]{6,5,1,4,3,0,2:T(8,128)(2,1)S(1)}, bf16[4,1,1,3,3,128,128]{6,5,1,4,3,0,2:T(8,128)(2,1)}, u32[]{:S(2)}) copy-start(bf16[4,1,1,3,3,128,128]{6,5,1,4,3,0,2:T(8,128)(2,1)} %get-tuple-element.404) | copy-start | bytes 3538948
  341.2 19.5 %collective-permute-start.6 = (bf16[2,1,2,128,384]{4,3,2,0,1:T(8,128)(2,1)}, bf16[2,1,2,128,384]{4,3,2,0,1:T(8,128)(2,1)}, u32[]{:S(2)}, u32[]{:S(2)}) collective-permute-start(bf16[2,1,2,128,384]{4,3,2,0,1:T(8,128)(2,1)} %get-tuple-element.411), channel_id=1, source_target_pairs={{0,4},{4,8},{8,12},{12,16},{16,20},{20,24},{24,28},{1,5},{5,9},{9,... | collective-permute-start | bytes 1179656 | tf_op jit(solution)/shard_map/ppermute | solution.py:12
  357.2 9.9 %collective-permute-start.7 = (bf16[2,1,2,128,384]{4,3,2,0,1:T(8,128)(2,1)}, bf16[2,1,2,128,384]{4,3,2,0,1:T(8,128)(2,1)S(1)}, u32[]{:S(2)}, u32[]{:S(2)}) collective-permute-start(bf16[2,1,2,128,384]{4,3,2,0,1:T(8,128)(2,1)} %get-tuple-element.410), channel_id=1, source_target_pairs={{4,0},{8,4},{12,8},{16,12},{20,16},{24,20},{28,24},{5,1},{9,5},{13... | collective-permute-start | bytes 1179656 | tf_op jit(solution)/shard_map/ppermute | solution.py:12
Sparse Core Ops, SparseCore 0:
  9.8 174.3 all-gather.1
